TPU v7x, 32 devices: a whole 2x2x4 slice. The times are simulated.
32 devices in a mesh: dp: 4 (over y, x), expert: 2 (over core), tensor: 4 (over z).
Axes of the slice: x: 2, y: 2, z: 4, core: 2. Of those that a mesh axis runs over, the one named last changes fastest.
Arguments:
- tokens: bfloat16 [4096, 2048], P(('dp', 'expert', 'tensor')), may hold values from -6 to 6
- norm_gain: float32 [2048], replicated, may hold values from 0.1 to 1.9
- expert_ids: int32 [4096, 8], P(('dp', 'expert', 'tensor')), may hold values from 0 to 31, all different within a row; in each aligned block of 128 rows (0 to 127, 128 to 255, ...) at most 64 rows name the same one
- gate_weights: float32 [4096, 8], P(('dp', 'expert', 'tensor')), may hold values from 0.03 to 0.4
- w_in: bfloat16 [32, 2048, 1536], P(('dp', 'expert', 'tensor')), may hold values from -1.875 to 1.875, as said below
- scale_in: float32 [32, 16, 12], P(('dp', 'expert', 'tensor')), may hold values from 0.03 to 0.12
- w_out: bfloat16 [32, 768, 2048], P(('dp', 'expert', 'tensor')), may hold values from -1.875 to 1.875, as said below
- scale_out: float32 [32, 6, 16], P(('dp', 'expert', 'tensor')), may hold values from 0.02 to 0.08
- w_sync: bfloat16 [2048, 2, 2048], P(None, None, 'tensor'), may hold values from -0.125 to 0.125
- head_weight: float32 [16], P('tensor'), may hold values from -3 to 3
- frame_rows: int32 [8, 2, 256], P(('dp', 'expert')), may hold values from 0 to 511, as said below
- lag_offsets: int32 [21], replicated, may hold values from -32 to 32, as said below
Outputs:
- mixed: bfloat16 [4096, 2048], P(('dp', 'expert', 'tensor'))
- sync_logits: float32 [8, 21], P(('dp', 'expert'))
Inputs may be any that keep to these rules, and one draw needn't show every extreme that they name: `expert_ids`: in each aligned block of 128 rows (the rows of one device) no expert is named by more than 64 of the block's choices; the choices of a row are different. `w_in`: every entry is an e4m3 value: a sign times (1 + m / 8) times 2 to the e, with whole m of 0 to 7 and e of -3 to 0. `w_out`: every entry is an e4m3 value: a sign times (1 + m / 8) times 2 to the e, with whole m of 0 to 7 and e of -3 to 0. `frame_rows`: for each clip the audio rows and the video rows together are each of 0 to 511 once. `lag_offsets`: 21 different lags in increasing order; the first is -32 and the last 32.
All inputs are finite; a program needn't handle non-finite values.
Results may differ from a plain program's by a relative error of at most 0.0035.
The roundings to bfloat16 on the way count: a program that leaves them out, or rounds other values in their place, can miss the bound.
Values may be sent and summed in bfloat16 or wider, within the bound.
No kernel may reach another device: no remote copies, remote signals or barrier semaphores. Data moves between devices by JAX's collectives and lax.ppermute only.
A program may use at most 128 MiB of HBM per device.

v0:
```python
import jax
import jax.numpy as jnp
from jax import lax
from jax.sharding import PartitionSpec as P


def dequant(weights, scales):
    block = weights.shape[0] // scales.shape[0]
    full = jnp.repeat(jnp.repeat(scales, block, axis=0), block, axis=1)
    return (weights.astype(jnp.float32) * full).astype(jnp.bfloat16)


def shards(
    tokens,
    norm_gain,
    expert_ids,
    gate_weights,
    w_in,
    scale_in,
    w_out,
    scale_out,
    w_sync,
    head_weight,
    frame_rows,
    lag_offsets,
):
    rows, width = tokens.shape
    top = expert_ids.shape[1]
    lines = lax.axis_size("tensor")
    plane = lax.axis_size(("dp", "expert"))
    experts_all = plane * lines * w_in.shape[0]
    most = 2 * rows * top // experts_all
    cap = lines * most
    here = lax.axis_index("tensor")
    x_float = tokens.astype(jnp.float32)
    normed = (
        x_float * lax.rsqrt(jnp.mean(x_float * x_float, axis=-1, keepdims=True) + 1e-06) * norm_gain
    ).astype(jnp.bfloat16)

    flat_ids = expert_ids.reshape(-1)
    pair_count = rows * top
    onehot = (flat_ids[:, None] == jnp.arange(experts_all, dtype=jnp.int32)[None, :]).astype(
        jnp.bfloat16
    )
    pair_index = jnp.arange(pair_count, dtype=jnp.int32)
    earlier = (pair_index[None, :] < pair_index[:, None]).astype(jnp.bfloat16)
    before = jnp.dot(earlier, onehot, preferred_element_type=jnp.float32)
    slots = jnp.sum(before * onehot.astype(jnp.float32), axis=1).reshape(rows, top)
    gate = gate_weights.astype(jnp.float32)
    gate_top = lax.reduce_precision(gate, exponent_bits=8, mantissa_bits=7)
    routing = jnp.concatenate(
        [
            expert_ids.astype(jnp.bfloat16),
            slots.astype(jnp.bfloat16),
            gate_top.astype(jnp.bfloat16),
            (gate - gate_top).astype(jnp.bfloat16),
        ],
        axis=1,
    )
    half = width // 2
    extra = rows * 4 * top // half
    padded = rows + 16
    packed = jnp.concatenate(
        [
            normed[:, :half],
            routing.reshape(extra, half),
            jnp.zeros((padded - rows - extra, half), jnp.bfloat16),
        ],
        axis=0,
    )
    line_a = lax.all_gather(packed, "tensor", axis=0, tiled=False)
    line_b = lax.all_gather(normed[:, half:], "tensor", axis=0, tiled=False)
    line_routing = line_a[:, rows : rows + extra, :].reshape(lines, rows, 4 * top)
    ids_l = line_routing[:, :, :top].astype(jnp.int32)
    slot_l = line_routing[:, :, top : 2 * top].astype(jnp.int32)
    gate_hi = line_routing[:, :, 2 * top : 3 * top].astype(jnp.float32)
    gate_lo = line_routing[:, :, 3 * top :].astype(jnp.float32)
    mine = (ids_l % lines) == here
    target = jnp.where(mine, (ids_l // lines) * most + slot_l, -1)
    slot_ids = jnp.arange(plane * most, dtype=jnp.int32)
    match = target[:, None, :, :] == slot_ids[None, :, None, None]
    order = (here + jnp.arange(lines, dtype=jnp.int32)) % lines
    select = jnp.any(match, axis=3).astype(jnp.bfloat16).reshape(lines, plane, most, rows)
    select_rel = jnp.take(select, order[1:], axis=0)
    weight_hi = jnp.sum(jnp.where(match, gate_hi[:, None, :, :], 0.0), axis=3)
    weight_lo = jnp.sum(jnp.where(match, gate_lo[:, None, :, :], 0.0), axis=3)
    weight_hi = weight_hi.astype(jnp.bfloat16).reshape(lines, plane, most, rows)
    weight_lo = weight_lo.astype(jnp.bfloat16).reshape(lines, plane, most, rows)
    line_parts = [
        jnp.take(line_a[:, :rows], order[1:], axis=0),
        jnp.take(line_b, order[1:], axis=0),
    ]
    own_target = jnp.where(
        (expert_ids % lines) == here,
        (expert_ids // lines) * most + slots.astype(jnp.int32),
        -1,
    )
    own_select = jnp.any(
        own_target[None, :, :] == slot_ids[:, None, None], axis=2
    ).astype(jnp.bfloat16)
    gate_up = dequant(w_in[0], scale_in[0])
    down_proj = dequant(w_out[0], scale_out[0])
    hidden_width = down_proj.shape[0]
    group = ("dp", "expert")

    def send(part, depth):
        moved = lax.all_to_all(
            part.reshape(plane, depth, part.shape[-1]), group, split_axis=0, concat_axis=0, tiled=True
        )
        return moved.reshape(plane * depth, part.shape[-1])

    own_block = send(
        jnp.dot(own_select, normed, preferred_element_type=jnp.float32).astype(jnp.bfloat16), most
    )
    blocks = [
        send(
            jnp.einsum(
                "dpsr,drD->pdsD", select_rel, line_parts[h], preferred_element_type=jnp.float32
            ).astype(jnp.bfloat16),
            cap - most,
        )
        for h in range(2)
    ]
    def activate(mixed_in):
        return (jax.nn.silu(mixed_in[:, :hidden_width]) * mixed_in[:, hidden_width:]).astype(
            jnp.bfloat16
        )

    own_hidden = activate(jnp.dot(own_block, gate_up, preferred_element_type=jnp.float32))
    rest_hidden = activate(
        jnp.dot(blocks[0], gate_up[:half], preferred_element_type=jnp.float32)
        + jnp.dot(blocks[1], gate_up[half:], preferred_element_type=jnp.float32)
    )
    hidden = jnp.concatenate(
        [
            own_hidden.reshape(plane, 1, most, hidden_width),
            rest_hidden.reshape(plane, lines - 1, most, hidden_width),
        ],
        axis=1,
    )
    hidden = jnp.take(
        hidden, (jnp.arange(lines, dtype=jnp.int32) - here) % lines, axis=1
    ).reshape(plane * cap, hidden_width)
    mixed_parts = []
    scattered = None
    cuts = [0, width * 5 // 8, width]
    for h in range(2):
        output = jnp.dot(
            hidden, down_proj[:, cuts[h] : cuts[h + 1]], preferred_element_type=jnp.float32
        ).astype(jnp.bfloat16)
        if scattered is not None:
            scattered, output = lax.optimization_barrier((scattered, output))
        back = send(output, cap)
        back = back.reshape(plane, lines, most, cuts[h + 1] - cuts[h])
        partial = jnp.einsum(
            "bpsr,pbsd->brd", weight_hi, back, preferred_element_type=jnp.float32
        ) + jnp.einsum("bpsr,pbsd->brd", weight_lo, back, preferred_element_type=jnp.float32)
        scattered = partial.reshape(lines * rows, cuts[h + 1] - cuts[h])
        mixed_parts.append(scattered)
    for h in range(2):
        combined = lax.psum_scatter(mixed_parts[h], "tensor", scatter_dimension=0, tiled=True)
        mixed_parts[h] = x_float[:, cuts[h] : cuts[h + 1]] + combined
    mixed = jnp.concatenate(mixed_parts, axis=1).astype(jnp.bfloat16)

    local_sync = w_sync.reshape(width, -1)
    proj = jnp.dot(
        lax.all_gather(mixed, "tensor", axis=0, tiled=True),
        local_sync,
        preferred_element_type=jnp.float32,
    ).astype(jnp.bfloat16)
    half = proj.shape[1] // 2
    heads_here = head_weight.shape[0]
    head_size = half // heads_here
    frames = frame_rows.shape[2]
    clip_len = proj.shape[0]
    clip_index = jnp.arange(clip_len, dtype=jnp.int32)
    pick_audio = (frame_rows[0, 0][:, None] == clip_index[None, :]).astype(jnp.bfloat16)
    pick_video = (frame_rows[0, 1][:, None] == clip_index[None, :]).astype(jnp.bfloat16)
    audio = (
        jnp.dot(pick_audio, proj[:, :half], preferred_element_type=jnp.float32)
        .astype(jnp.bfloat16)
        .reshape(frames, heads_here, head_size)
    )
    video = (
        jnp.dot(pick_video, proj[:, half:], preferred_element_type=jnp.float32)
        .astype(jnp.bfloat16)
        .reshape(frames, heads_here, head_size)
    )
    grams = jnp.einsum("thd,shd->hts", audio, video, preferred_element_type=jnp.float32)
    times = jnp.arange(frames, dtype=jnp.int32)
    offsets = times[None, :] - times[:, None]
    diagonal = (
        (offsets[None, :, :] == lag_offsets[:, None, None])
        .astype(jnp.float32)
        .reshape(lag_offsets.shape[0], frames * frames)
    )
    sums = lax.dot_general(
        grams.reshape(heads_here, frames * frames),
        diagonal,
        (((1,), (1,)), ((), ())),
        precision=lax.Precision.HIGHEST,
        preferred_element_type=jnp.float32,
    )
    counts = (frames - jnp.abs(lag_offsets)).astype(jnp.float32)
    score = sums / jnp.sqrt(counts * head_size)[None, :]
    partial_logits = jnp.sum(head_weight[:, None] * score, axis=0)
    sync_logits = partial_logits
    step = 1
    while step < lines:
        pairs = [(i, i ^ step) for i in range(lines)]
        sync_logits = sync_logits + lax.ppermute(sync_logits, "tensor", pairs)
        step *= 2
    return (mixed, sync_logits[None, :])


def solution(mesh):
    return jax.shard_map(
        shards,
        mesh=mesh,
        in_specs=(
            P(("dp", "expert", "tensor"), None),
            P(),
            P(("dp", "expert", "tensor"), None),
            P(("dp", "expert", "tensor"), None),
            P(("dp", "expert", "tensor"), None, None),
            P(("dp", "expert", "tensor"), None, None),
            P(("dp", "expert", "tensor"), None, None),
            P(("dp", "expert", "tensor"), None, None),
            P(None, None, "tensor"),
            P("tensor"),
            P(("dp", "expert"), None, None),
            P(),
        ),
        out_specs=(P(("dp", "expert", "tensor"), None), P(("dp", "expert"), None)),
        check_vma=False,
    )
```

profile of v0, /device:TPU:0, one launch (start us, length us, event | category | flops | bytes accessed | tf_op | source)
XLA Modules:
  0.0 405.8 jit_solution(16913383712554410197)
XLA Ops:
  17.8 5.2 %all-to-all-start = ((bf16[8,64,2048]{2,1,0:T(8,128)(2,1)}), bf16[8,64,2048]{2,1,0:T(8,128)(2,1)}, u32[]{:S(2)}, u32[]{:S(2)}) async-start(bf16[8,64,2048]{2,1,0:T(8,128)(2,1)} %bitcast.2), calls=%async_computation | async-start | bytes 4194304 | tf_op jit(solution)/shard_map/all_to_all | solution.py:107
  23.0 24.9 %all-gather.8.cloned.1.call-done = bf16[576,1024]{1,0:T(8,128)(2,1)} async-done(((bf16[144,1024]{1,0:T(8,128)(2,1)}), bf16[576,1024]{1,0:T(8,128)(2,1)}) %all-gather.8.cloned.1.call-update) | async-done | bytes 1179664 | tf_op jit(solution)/shard_map/all_gather | solution.py:71
  59.2 4.4 %all-to-all-start.1 = ((bf16[8,192,1024]{2,1,0:T(8,128)(2,1)}), bf16[8,192,1024]{2,1,0:T(8,128)(2,1)}, u32[]{:S(2)}, u32[]{:S(2)}) async-start(bf16[8,192,1024]{2,1,0:T(8,128)(2,1)} %bitcast.12), calls=%async_computation.1 | async-start | bytes 6291456 | tf_op jit(solution)/shard_map/all_to_all | solution.py:107
  63.7 12.1 %all-gather.10.cloned.1.call-start = ((), (), s32[]{:S(2)}) async-start(), calls=%async_computation.11 | async-start | bytes 1310720 | tf_op jit(solution)/shard_map/all_gather | solution.py:72
  75.8 8.7 %copy.107 = bf16[1,2048,1536]{1,2,0:T(8,128)(2,1)} copy(bf16[1,2048,1536]{2,1,0:T(8,128)(2,1)} %param.18) | data formatting | bytes 12582912 | tf_op args[4]
  84.9 7.8 %fusion = bf16[2048,1536]{0,1:T(8,128)(2,1)} fusion(f32[2048,12]{0,1:T(8,128)S(1)} %bitcast.149, bf16[1,2048,1536]{1,2,0:T(8,128)(2,1)} %copy.107), kind=kLoop, calls=%fused_computation.5 | loop fusion | flops 9437184 | bytes 12681216 | tf_op jit(solution)/shard_map/convert_element_type | solution.py:10
  92.8 4.5 %multiply_convert_fusion = bf16[2048,12,128]{0,2,1:T(8,128)(2,1)} fusion(f32[2048,12]{0,1:T(8,128)S(1)} %bitcast.150, bf16[2048,12,128]{0,2,1:T(8,128)(2,1)S(1)} %bitcast.124), kind=kLoop, calls=%fused_computation.6 | loop fusion | flops 9437184 | bytes 12681216 | tf_op jit(solution)/shard_map/convert_element_type | solution.py:10
  97.4 5.6 %all-gather.10.cloned.1.call-done = bf16[512,1024]{1,0:T(8,128)(2,1)} async-done(((bf16[128,1024]{1,0:T(8,128)(2,1)}), bf16[512,1024]{1,0:T(8,128)(2,1)}) %all-gather.10.cloned.1.call-update) | async-done | bytes 1048592 | tf_op jit(solution)/shard_map/all_gather | solution.py:72
  113.7 4.1 %fusion.2 = bf16[768,2048]{1,0:T(8,128)(2,1)} fusion(f32[96,8,16,128]{3,2,1,0:T(8,128)S(1)} %bitcast.127, bf16[1,768,2048]{2,1,0:T(8,128)(2,1)S(1)} %copy-done.2), kind=kLoop, calls=%fused_computation.14 | loop fusion | flops 4718592 | bytes 12582912 | tf_op jit(solution)/shard_map/convert_element_type | solution.py:10
  117.8 5.2 %fusion.99 = f32[512,1536]{1,0:T(8,128)S(1)} fusion(bf16[512,2048]{1,0:T(8,128)(2,1)} %bitcast.3, bf16[2048,1536]{0,1:T(8,128)(2,1)S(1)} %bitcast.140), kind=kOutput, calls=%fused_computation.159 | convolution fusion | flops 3221225472 | bytes 11534336 | tf_op jit(solution)/shard_map/dot_general | solution.py:129
  124.4 9.6 %fusion.21 = f32[1536,1536]{1,0:T(8,128)} fusion(bf16[1536,1024]{1,0:T(8,128)(2,1)} %bitcast.13, bf16[2048,1536]{0,1:T(8,128)(2,1)S(1)} %bitcast.137), kind=kOutput, calls=%fused_computation.30 | convolution fusion | flops 4831838208 | bytes 15728640 | tf_op jit(solution)/shard_map/dot_general | solution.py:131
  134.0 15.7 %all-to-all-done.2 = bf16[8,192,1024]{2,1,0:T(8,128)(2,1)S(1)} async-done(((bf16[8,192,1024]{2,1,0:T(8,128)(2,1)}), bf16[8,192,1024]{2,1,0:T(8,128)(2,1)S(1)}, u32[]{:S(2)}, u32[]{:S(2)}) %all-to-all-start.2) | async-done | bytes 3145760 | tf_op jit(solution)/shard_map/all_to_all | solution.py:107
  149.7 8.6 %convolution_add_fusion = f32[1536,1536]{1,0:T(8,128)S(1)} fusion(f32[1536,1536]{1,0:T(8,128)} %fusion.21, bf16[1536,1024]{1,0:T(8,128)(2,1)S(1)} %bitcast.144, bf16[2048,1536]{0,1:T(8,128)(2,1)} %fusion), kind=kOutput, calls=%fused_computation.7 | convolution fusion | flops 4834197504 | bytes 25165824 | tf_op jit(solution)/shard_map/dot_general | solution.py:132
  167.1 6.0 %convolution_convert_fusion = bf16[2048,1280]{1,0:T(8,128)(2,1)} fusion(bf16[2048,768]{1,0:T(8,128)(2,1)S(1)} %bitcast_select_fusion, bf16[768,2048]{1,0:T(8,128)(2,1)S(1)} %copy-done.3), kind=kOutput, calls=%fused_computation.12 | convolution fusion | flops 4029153280 | bytes 10354688 | tf_op jit(solution)/shard_map/dot_general | solution.py:148
  173.1 4.7 %all-to-all-start.3 = ((bf16[8,256,1280]{2,1,0:T(8,128)(2,1)}), bf16[8,256,1280]{2,1,0:T(8,128)(2,1)}, u32[]{:S(2)}, u32[]{:S(2)}) async-start(bf16[8,256,1280]{2,1,0:T(8,128)(2,1)} %bitcast.141), calls=%async_computation.3 | async-start | bytes 10485760 | tf_op jit(solution)/shard_map/all_to_all | solution.py:107
  178.2 6.0 %select_reduce_fusion.1 = (bf16[4,512,128]{2,1,0:T(8,128)(2,1)S(1)}, bf16[4,512,128]{2,1,0:T(8,128)(2,1)S(1)}) fusion(f32[4,128,8]{1,2,0:T(8,128)S(1)} %convert_element_type.163, s32[4,128,8]{1,2,0:T(8,128)S(1)} %copy.100, f32[4,128,8]{1,2,0:T(8,128)S(1)} %convert_element_type.188), kind=kLoop, calls=%fused_computation.9 | loop fusion | flops 9961472 | bytes 1097728 | tf_op jit(solution)/shard_map/reduce_sum | solution.py:85
  184.2 54.0 %all-to-all-done.3 = bf16[8,256,1280]{2,1,0:T(8,128)(2,1)} async-done(((bf16[8,256,1280]{2,1,0:T(8,128)(2,1)}), bf16[8,256,1280]{2,1,0:T(8,128)(2,1)}, u32[]{:S(2)}, u32[]{:S(2)}) %all-to-all-start.3) | async-done | bytes 5242912 | tf_op jit(solution)/shard_map/all_to_all | solution.py:107
  241.6 4.9 %fusion.14 = f32[4,128,1280]{2,1,0:T(8,128)} fusion(f32[4,128,1280]{2,1,0:T(8,128)S(1)} %fusion.17, bf16[4,8,64,128]{3,2,1,0:T(8,128)(2,1)S(1)} %bitcast.132, bf16[8,4,64,1280]{3,2,1,0:T(8,128)(2,1)} %bitcast.29), kind=kOutput, calls=%fused_computation.27 | convolution fusion | flops 671744000 | bytes 11010048 | tf_op jit(solution)/shard_map/bpsr,pbsd->brd/dot_general | solution.py:155
  246.7 4.8 %convolution_convert_fusion.1 = bf16[2048,768]{1,0:T(8,128)(2,1)S(1)} fusion(bf16[2048,768]{1,0:T(8,128)(2,1)} %copy-done.1, bf16[768,2048]{1,0:T(8,128)(2,1)} %fusion.2), kind=kOutput, calls=%fused_computation.25 | convolution fusion | flops 2417491968 | bytes 7471104 | tf_op jit(solution)/shard_map/dot_general | solution.py:148
  251.6 40.3 %all_to_all.25 = bf16[8,256,768]{2,1,0:T(8,128)(2,1)S(1)} all-to-all(bf16[8,256,768]{2,1,0:T(8,128)(2,1)S(1)} %bitcast.145), channel_id=1, replica_groups=mesh['dp'=4,'expert'=2,'tensor'=4] {'dp','expert'}, dimensions={0} | all-to-all | bytes 6291456 | tf_op jit(solution)/shard_map/all_to_all | solution.py:107
  297.6 36.0 %reduce-scatter.5.cloned.1.call-done = f32[128,768]{1,0:T(8,128)} async-done(((f32[512,768]{1,0:T(8,128)}), f32[128,768]{1,0:T(8,128)}) %reduce-scatter.5.cloned.1.call-update) | async-done | bytes 393232 | tf_op jit(solution)/shard_map/reduce_scatter | solution.py:161
  335.6 5.3 %copy.134 = bf16[256,8,2,512]{3,1,2,0:T(8,128)(2,1)} copy(bf16[256,8,2,512]{3,2,1,0:T(2,128)(2,1)} %bitcast.142) | data formatting | bytes 8388608
  341.0 39.6 %all-gather.6.cloned.1.call-done = bf16[512,2048]{1,0:T(8,128)(2,1)} async-done(((bf16[128,2048]{1,0:T(8,128)(2,1)}), bf16[512,2048]{1,0:T(8,128)(2,1)}) %all-gather.6.cloned.1.call-update) | async-done | bytes 2097168 | tf_op jit(solution)/shard_map/all_gather | solution.py:167
  380.6 5.2 %convolution_convert_fusion.3 = bf16[512,1024]{1,0:T(8,128)(2,1)S(1)} fusion(bf16[512,2048]{1,0:T(8,128)(2,1)} %all-gather.6.cloned.1.call-done, bf16[2048,1024]{1,0:T(8,128)(2,1)} %bitcast.143), kind=kOutput, calls=%fused_computation.49 | convolution fusion | flops 2148007936 | bytes 7340032 | tf_op jit(solution)/shard_map/dot_general | solution.py:166
  (131 shorter events, 68.0 us)
Async XLA Ops:
  7.2 40.8 %all-gather.8.cloned.1.call-start = ((), (), s32[]{:S(2)}) async-start(), calls=%async_computation.10 | async-start | bytes 1474560 | tf_op jit(solution)/shard_map/all_gather | solution.py:71
  17.8 41.4 %all-to-all-start = ((bf16[8,64,2048]{2,1,0:T(8,128)(2,1)}), bf16[8,64,2048]{2,1,0:T(8,128)(2,1)}, u32[]{:S(2)}, u32[]{:S(2)}) async-start(bf16[8,64,2048]{2,1,0:T(8,128)(2,1)} %bitcast.2), calls=%async_computation | async-start | bytes 4194304 | tf_op jit(solution)/shard_map/all_to_all | solution.py:107
  59.2 48.8 %all-to-all-start.1 = ((bf16[8,192,1024]{2,1,0:T(8,128)(2,1)}), bf16[8,192,1024]{2,1,0:T(8,128)(2,1)}, u32[]{:S(2)}, u32[]{:S(2)}) async-start(bf16[8,192,1024]{2,1,0:T(8,128)(2,1)} %bitcast.12), calls=%async_computation.1 | async-start | bytes 6291456 | tf_op jit(solution)/shard_map/all_to_all | solution.py:107
  63.7 39.3 %all-gather.10.cloned.1.call-start = ((), (), s32[]{:S(2)}) async-start(), calls=%async_computation.11 | async-start | bytes 1310720 | tf_op jit(solution)/shard_map/all_gather | solution.py:72
  75.8 8.8 %copy-start.5 = (f32[1,16,12]{1,0,2:T(1,128)S(1)}, f32[1,16,12]{1,0,2:T(1,128)}, u32[]{:S(2)}) copy-start(f32[1,16,12]{1,0,2:T(1,128)} %param.19) | copy-start | bytes 2308
  75.8 9.1 %copy-start.6 = (f32[1,6,16]{2,0,1:T(1,128)S(1)}, f32[1,6,16]{2,0,1:T(1,128)}, u32[]{:S(2)}) copy-start(f32[1,6,16]{2,0,1:T(1,128)} %param.21) | copy-start | bytes 1156
  84.9 7.9 %slice-start = ((s8[6291456]{0:T(1024)(128)(4,1)}), s8[4194304]{0:T(1024)(128)(4,1)S(1)}, s32[]{:S(2)}) async-start(s8[6291456]{0:T(1024)(128)(4,1)} %bitcast.122), calls=%async_computation.12 | async-start | bytes 8388608
  84.9 7.9 %slice-start.1 = ((s8[6291456]{0:T(1024)(128)(4,1)}), s8[2097152]{0:T(1024)(128)(4,1)S(1)}, s32[]{:S(2)}) async-start(s8[6291456]{0:T(1024)(128)(4,1)} %bitcast.122), calls=%async_computation.13 | async-start | bytes 4194304
  108.1 41.7 %all-to-all-start.2 = ((bf16[8,192,1024]{2,1,0:T(8,128)(2,1)}), bf16[8,192,1024]{2,1,0:T(8,128)(2,1)S(1)}, u32[]{:S(2)}, u32[]{:S(2)}) async-start(bf16[8,192,1024]{2,1,0:T(8,128)(2,1)} %bitcast.20), calls=%async_computation.2 | async-start | bytes 6291456 | tf_op jit(solution)/shard_map/all_to_all | solution.py:107
  111.9 5.9 %slice-start.4 = ((s8[6291456]{0:T(1024)(128)(4,1)}), s8[4194304]{0:T(1024)(128)(4,1)S(1)}, s32[]{:S(2)}) async-start(s8[6291456]{0:T(1024)(128)(4,1)} %bitcast.138), calls=%async_computation.16 | async-start | bytes 8388608
  113.7 4.1 %slice-start.5 = ((s8[6291456]{0:T(1024)(128)(4,1)}), s8[2097152]{0:T(1024)(128)(4,1)S(1)}, s32[]{:S(2)}) async-start(s8[6291456]{0:T(1024)(128)(4,1)} %bitcast.138), calls=%async_computation.17 | async-start | bytes 4194304
  113.7 10.7 %slice-start.2 = ((s8[6291456]{0:T(1024)(128)(4,1)}), s8[2097152]{0:T(1024)(128)(4,1)S(1)}, s32[]{:S(2)}) async-start(s8[6291456]{0:T(1024)(128)(4,1)} %bitcast.136), calls=%async_computation.14 | async-start | bytes 4194304
  117.8 6.6 %slice-start.3 = ((s8[6291456]{0:T(1024)(128)(4,1)}), s8[4194304]{0:T(1024)(128)(4,1)S(1)}, s32[]{:S(2)}) async-start(s8[6291456]{0:T(1024)(128)(4,1)} %bitcast.136), calls=%async_computation.15 | async-start | bytes 8388608
  158.4 2.0 copy-start.4
  167.1 6.0 %copy-start.1 = (bf16[2048,768]{1,0:T(8,128)(2,1)}, bf16[2048,768]{1,0:T(8,128)(2,1)S(1)}, u32[]{:S(2)}) copy-start(bf16[2048,768]{1,0:T(8,128)(2,1)S(1)} %bitcast_select_fusion) | copy-start | bytes 9437188
  173.1 65.0 %all-to-all-start.3 = ((bf16[8,256,1280]{2,1,0:T(8,128)(2,1)}), bf16[8,256,1280]{2,1,0:T(8,128)(2,1)}, u32[]{:S(2)}, u32[]{:S(2)}) async-start(bf16[8,256,1280]{2,1,0:T(8,128)(2,1)} %bitcast.141), calls=%async_computation.3 | async-start | bytes 10485760 | tf_op jit(solution)/shard_map/all_to_all | solution.py:107
  177.8 118.7 %reduce-scatter.3.cloned.1.call-start = ((), (), s32[]{:S(2)}) async-start(), calls=%async_computation.7 | async-start | bytes 3276800 | tf_op jit(solution)/shard_map/reduce_scatter | solution.py:161
  246.5 87.1 %reduce-scatter.5.cloned.1.call-start = ((), (), s32[]{:S(2)}) async-start(), calls=%async_computation.8 | async-start | bytes 1966080 | tf_op jit(solution)/shard_map/reduce_scatter | solution.py:161
  292.5 1.9 copy-start
  294.4 86.2 %all-gather.6.cloned.1.call-start = ((), (), s32[]{:S(2)}) async-start(), calls=%async_computation.9 | async-start | bytes 2621440 | tf_op jit(solution)/shard_map/all_gather | solution.py:167
  335.6 5.4 %copy-start.8 = (s32[21]{0:T(128)S(1)}, s32[21]{0:T(128)}, u32[]{:S(2)}) copy-start(s32[21]{0:T(128)} %param.25) | copy-start | bytes 256
  335.6 5.4 %copy-start.7 = (s32[1,2,256]{2,1,0:T(2,128)S(1)}, s32[1,2,256]{2,1,0:T(2,128)}, u32[]{:S(2)}) copy-start(s32[1,2,256]{2,1,0:T(2,128)} %param.24) | copy-start | bytes 6148
  390.5 3.6 collective-permute-start
  394.2 4.4 %collective-permute-start.1 = (f32[21]{0:T(128)S(1)}, f32[21]{0:T(128)S(1)}, u32[]{:S(2)}, u32[]{:S(2)}) collective-permute-start(f32[21]{0:T(128)S(1)} %add.131), channel_id=1, source_target_pairs={{0,2},{1,3},{2,0},{3,1},{4,6},{5,7},{6,4},{7,5},{8,10},{9,11},{10,... | collective-permute-start | bytes 260 | tf_op jit(solution)/shard_map/ppermute | solution.py:211
  (3 other events, 4.8 us)
Sparse Core Ops, SparseCore 0:
  14.7 33.1 all-gather.7
  75.9 27.0 all-gather.9
  246.6 49.8 reduce-scatter.2
  298.6 34.9 reduce-scatter.4
  335.7 44.8 all-gather.5
where the time goes:
time: 411 us; the launch traced here: 406 us
  waiting for transfers between devices  185 us (45%)
  matrix products  59.6 us (15%)
  other arithmetic  40.7 us (10%)
  blocking collectives  40.3 us (10%)
  local copies, waits for them, and re-layouts  34.4 us (8%)
  starting transfers between devices  31.6 us (8%)
  between operations  14.5 us (4%)
    all_to_all x4, waiting for transfers between devices, send(): lax.all_to_all(part.reshape(plane, depth, part.shape[-1]), group, split_a...  69.7 us
    all_to_all x1, blocking collectives, send(): lax.all_to_all(part.reshape(plane, depth, part.shape[-1]), group, split_a...  40.3 us
    all_gather x1, waiting for transfers between devices, shards(): lax.all_gather(mixed, 'tensor', axis=0, tiled=True)  39.6 us
    reduce_scatter x2, waiting for transfers between devices, shards(): lax.psum_scatter(mixed_parts[h], 'tensor', scatter_dimension=0, tiled=True)  37.9 us
    all_gather x1, waiting for transfers between devices, shards(): line_a = lax.all_gather(packed, 'tensor', axis=0, tiled=False)  24.9 us
    all_to_all x4, starting transfers between devices, send(): lax.all_to_all(part.reshape(plane, depth, part.shape[-1]), group, split_a...  18.1 us
    unnamed x42, local copies, waits for them, and re-layouts  16.5 us
    convert_element_type x3, other arithmetic, dequant(): return (weights.astype(jnp.float32) * full).astype(jnp.bfloat16)  16.4 us
  transfers between devices with their start and end apart: 11, of which 9 were waited for; matrix products, arithmetic and copies ran while one was open for 21% of the time, Pallas kernels for 0%

commit v1 on v0

--- a/solution.py
+++ b/solution.py
@@ -143,7 +143,7 @@
     ).reshape(plane * cap, hidden_width)
     mixed_parts = []
     scattered = None
-    cuts = [0, width * 5 // 8, width]
+    cuts = [0, width * 9 // 16, width]
     for h in range(2):
         output = jnp.dot(
             hidden, down_proj[:, cuts[h] : cuts[h + 1]], preferred_element_type=jnp.float32

time: 411 us -> 409 us (level)
  waiting for transfers between devices: 185 us -> 177 us
  blocking collectives: 40.3 us -> 45.9 us
    all_to_all x1, blocking collectives: 40.3 us -> 45.9 us  [send(): lax.all_to_all(part.reshape(plane, depth, part.shape[-1]), group, split_a...]
    all_to_all x4, waiting for transfers between devices: 69.7 us -> 64.1 us  [send(): lax.all_to_all(part.reshape(plane, depth, part.shape[-1]), group, split_a...]
  transfers between devices with their start and end apart: 11 -> 11, of which waited for: 9 -> 8; matrix products, arithmetic and copies ran while one was open for 21% -> 21% of each run, Pallas kernels for 0% -> 0%
where the time goes in v1:
time: 409 us; the launch traced here: 405 us
  waiting for transfers between devices  177 us (43%)
  matrix products  60.3 us (15%)
  blocking collectives  45.9 us (11%)
  other arithmetic  40.7 us (10%)
  local copies, waits for them, and re-layouts  34.4 us (8%)
  starting transfers between devices  31.6 us (8%)
  between operations  14.5 us (4%)
    all_to_all x4, waiting for transfers between devices, send(): lax.all_to_all(part.reshape(plane, depth, part.shape[-1]), group, split_a...  64.1 us
    all_to_all x1, blocking collectives, send(): lax.all_to_all(part.reshape(plane, depth, part.shape[-1]), group, split_a...  45.9 us
    all_gather x1, waiting for transfers between devices, shards(): lax.all_gather(mixed, 'tensor', axis=0, tiled=True)  39.8 us
    reduce_scatter x2, waiting for transfers between devices, shards(): lax.psum_scatter(mixed_parts[h], 'tensor', scatter_dimension=0, tiled=True)  35.9 us
    all_gather x1, waiting for transfers between devices, shards(): line_a = lax.all_gather(packed, 'tensor', axis=0, tiled=False)  24.9 us
    all_to_all x4, starting transfers between devices, send(): lax.all_to_all(part.reshape(plane, depth, part.shape[-1]), group, split_a...  18 us
    unnamed x42, local copies, waits for them, and re-layouts  16.5 us
    convert_element_type x3, other arithmetic, dequant(): return (weights.astype(jnp.float32) * full).astype(jnp.bfloat16)  16.4 us
  transfers between devices with their start and end apart: 11, of which 8 were waited for; matrix products, arithmetic and copies ran while one was open for 21% of the time, Pallas kernels for 0%

profile of v1, /device:TPU:0, one launch (start us, length us, event | category | flops | bytes accessed | tf_op | source)
XLA Modules:
  0.0 404.7 jit_solution(2369902317456169106)
XLA Ops:
  17.8 5.2 %all-to-all-start = ((bf16[8,64,2048]{2,1,0:T(8,128)(2,1)}), bf16[8,64,2048]{2,1,0:T(8,128)(2,1)}, u32[]{:S(2)}, u32[]{:S(2)}) async-start(bf16[8,64,2048]{2,1,0:T(8,128)(2,1)} %bitcast.2), calls=%async_computation | async-start | bytes 4194304 | tf_op jit(solution)/shard_map/all_to_all | solution.py:107
  23.0 24.9 %all-gather.8.cloned.1.call-done = bf16[576,1024]{1,0:T(8,128)(2,1)} async-done(((bf16[144,1024]{1,0:T(8,128)(2,1)}), bf16[576,1024]{1,0:T(8,128)(2,1)}) %all-gather.8.cloned.1.call-update) | async-done | bytes 1179664 | tf_op jit(solution)/shard_map/all_gather | solution.py:71
  59.2 4.4 %all-to-all-start.1 = ((bf16[8,192,1024]{2,1,0:T(8,128)(2,1)}), bf16[8,192,1024]{2,1,0:T(8,128)(2,1)}, u32[]{:S(2)}, u32[]{:S(2)}) async-start(bf16[8,192,1024]{2,1,0:T(8,128)(2,1)} %bitcast.12), calls=%async_computation.1 | async-start | bytes 6291456 | tf_op jit(solution)/shard_map/all_to_all | solution.py:107
  63.7 12.1 %all-gather.10.cloned.1.call-start = ((), (), s32[]{:S(2)}) async-start(), calls=%async_computation.11 | async-start | bytes 1310720 | tf_op jit(solution)/shard_map/all_gather | solution.py:72
  75.8 8.7 %copy.107 = bf16[1,2048,1536]{1,2,0:T(8,128)(2,1)} copy(bf16[1,2048,1536]{2,1,0:T(8,128)(2,1)} %param.18) | data formatting | bytes 12582912 | tf_op args[4]
  84.9 7.8 %fusion = bf16[2048,1536]{0,1:T(8,128)(2,1)} fusion(f32[2048,12]{0,1:T(8,128)S(1)} %bitcast.149, bf16[1,2048,1536]{1,2,0:T(8,128)(2,1)} %copy.107), kind=kLoop, calls=%fused_computation.5 | loop fusion | flops 9437184 | bytes 12681216 | tf_op jit(solution)/shard_map/convert_element_type | solution.py:10
  92.8 4.5 %multiply_convert_fusion = bf16[2048,12,128]{0,2,1:T(8,128)(2,1)} fusion(f32[2048,12]{0,1:T(8,128)S(1)} %bitcast.150, bf16[2048,12,128]{0,2,1:T(8,128)(2,1)S(1)} %bitcast.126), kind=kLoop, calls=%fused_computation.6 | loop fusion | flops 9437184 | bytes 12681216 | tf_op jit(solution)/shard_map/convert_element_type | solution.py:10
  97.4 5.6 %all-gather.10.cloned.1.call-done = bf16[512,1024]{1,0:T(8,128)(2,1)} async-done(((bf16[128,1024]{1,0:T(8,128)(2,1)}), bf16[512,1024]{1,0:T(8,128)(2,1)}) %all-gather.10.cloned.1.call-update) | async-done | bytes 1048592 | tf_op jit(solution)/shard_map/all_gather | solution.py:72
  113.7 4.1 %fusion.2 = bf16[768,2048]{1,0:T(8,128)(2,1)} fusion(f32[96,8,16,128]{3,2,1,0:T(8,128)S(1)} %bitcast.127, bf16[1,768,2048]{2,1,0:T(8,128)(2,1)S(1)} %copy-done.2), kind=kLoop, calls=%fused_computation.14 | loop fusion | flops 4718592 | bytes 12582912 | tf_op jit(solution)/shard_map/convert_element_type | solution.py:10
  117.8 5.2 %fusion.99 = f32[512,1536]{1,0:T(8,128)S(1)} fusion(bf16[512,2048]{1,0:T(8,128)(2,1)} %bitcast.3, bf16[2048,1536]{0,1:T(8,128)(2,1)S(1)} %bitcast.140), kind=kOutput, calls=%fused_computation.159 | convolution fusion | flops 3221225472 | bytes 11534336 | tf_op jit(solution)/shard_map/dot_general | solution.py:129
  124.4 9.6 %fusion.25 = f32[1536,1536]{1,0:T(8,128)} fusion(bf16[1536,1024]{1,0:T(8,128)(2,1)} %bitcast.13, bf16[2048,1536]{0,1:T(8,128)(2,1)S(1)} %bitcast.137), kind=kOutput, calls=%fused_computation.34 | convolution fusion | flops 4831838208 | bytes 15728640 | tf_op jit(solution)/shard_map/dot_general | solution.py:131
  134.0 15.7 %all-to-all-done.2 = bf16[8,192,1024]{2,1,0:T(8,128)(2,1)S(1)} async-done(((bf16[8,192,1024]{2,1,0:T(8,128)(2,1)}), bf16[8,192,1024]{2,1,0:T(8,128)(2,1)S(1)}, u32[]{:S(2)}, u32[]{:S(2)}) %all-to-all-start.2) | async-done | bytes 3145760 | tf_op jit(solution)/shard_map/all_to_all | solution.py:107
  149.7 8.6 %convolution_add_fusion = f32[1536,1536]{1,0:T(8,128)S(1)} fusion(f32[1536,1536]{1,0:T(8,128)} %fusion.25, bf16[1536,1024]{1,0:T(8,128)(2,1)S(1)} %bitcast.145, bf16[2048,1536]{0,1:T(8,128)(2,1)} %fusion), kind=kOutput, calls=%fused_computation.7 | convolution fusion | flops 4834197504 | bytes 25165824 | tf_op jit(solution)/shard_map/dot_general | solution.py:132
  167.1 5.9 %convolution_convert_fusion = bf16[2048,1152]{1,0:T(8,128)(2,1)} fusion(bf16[2048,768]{1,0:T(8,128)(2,1)S(1)} %bitcast_select_fusion, bf16[768,2048]{1,0:T(8,128)(2,1)S(1)} %copy-done.3), kind=kOutput, calls=%fused_computation.12 | convolution fusion | flops 3626237952 | bytes 9633792 | tf_op jit(solution)/shard_map/dot_general | solution.py:148
  173.0 4.6 %all-to-all-start.3 = ((bf16[8,256,1152]{2,1,0:T(8,128)(2,1)}), bf16[8,256,1152]{2,1,0:T(8,128)(2,1)}, u32[]{:S(2)}, u32[]{:S(2)}) async-start(bf16[8,256,1152]{2,1,0:T(8,128)(2,1)} %bitcast.141), calls=%async_computation.3 | async-start | bytes 9437184 | tf_op jit(solution)/shard_map/all_to_all | solution.py:107
  178.1 6.0 %select_reduce_fusion.1 = (bf16[4,512,128]{2,1,0:T(8,128)(2,1)S(1)}, bf16[4,512,128]{2,1,0:T(8,128)(2,1)S(1)}) fusion(f32[4,128,8]{1,2,0:T(8,128)S(1)} %convert_element_type.163, s32[4,128,8]{1,2,0:T(8,128)S(1)} %copy.100, f32[4,128,8]{1,2,0:T(8,128)S(1)} %convert_element_type.188), kind=kLoop, calls=%fused_computation.9 | loop fusion | flops 9961472 | bytes 1097728 | tf_op jit(solution)/shard_map/reduce_sum | solution.py:85
  184.1 48.3 %all-to-all-done.3 = bf16[8,256,1152]{2,1,0:T(8,128)(2,1)} async-done(((bf16[8,256,1152]{2,1,0:T(8,128)(2,1)}), bf16[8,256,1152]{2,1,0:T(8,128)(2,1)}, u32[]{:S(2)}, u32[]{:S(2)}) %all-to-all-start.3) | async-done | bytes 4718624 | tf_op jit(solution)/shard_map/all_to_all | solution.py:107
  235.7 4.6 %fusion.14 = f32[4,128,1152]{2,1,0:T(8,128)} fusion(f32[4,128,1152]{2,1,0:T(8,128)S(1)} %fusion.17, bf16[4,8,64,128]{3,2,1,0:T(8,128)(2,1)S(1)} %bitcast.132, bf16[8,4,64,1152]{3,2,1,0:T(8,128)(2,1)} %bitcast.29), kind=kOutput, calls=%fused_computation.27 | convolution fusion | flops 604569600 | bytes 9961472 | tf_op jit(solution)/shard_map/bpsr,pbsd->brd/dot_general | solution.py:155
  240.5 5.7 %convolution_convert_fusion.1 = bf16[2048,896]{1,0:T(8,128)(2,1)S(1)} fusion(bf16[2048,768]{1,0:T(8,128)(2,1)} %copy-done.1, bf16[768,2048]{1,0:T(8,128)(2,1)} %fusion.2), kind=kOutput, calls=%fused_computation.25 | convolution fusion | flops 2820407296 | bytes 8192000 | tf_op jit(solution)/shard_map/dot_general | solution.py:148
  246.3 45.9 %all_to_all.25 = bf16[8,256,896]{2,1,0:T(8,128)(2,1)S(1)} all-to-all(bf16[8,256,896]{2,1,0:T(8,128)(2,1)S(1)} %bitcast.144), channel_id=1, replica_groups=mesh['dp'=4,'expert'=2,'tensor'=4] {'dp','expert'}, dimensions={0} | all-to-all | bytes 7340032 | tf_op jit(solution)/shard_map/all_to_all | solution.py:107
  296.4 35.9 %reduce-scatter.5.cloned.1.call-done = f32[128,896]{1,0:T(8,128)} async-done(((f32[512,896]{1,0:T(8,128)}), f32[128,896]{1,0:T(8,128)}) %reduce-scatter.5.cloned.1.call-update) | async-done | bytes 458768 | tf_op jit(solution)/shard_map/reduce_scatter | solution.py:161
  334.3 5.3 %copy.134 = bf16[256,8,2,512]{3,1,2,0:T(8,128)(2,1)} copy(bf16[256,8,2,512]{3,2,1,0:T(2,128)(2,1)} %bitcast.142) | data formatting | bytes 8388608
  339.7 39.8 %all-gather.6.cloned.1.call-done = bf16[512,2048]{1,0:T(8,128)(2,1)} async-done(((bf16[128,2048]{1,0:T(8,128)(2,1)}), bf16[512,2048]{1,0:T(8,128)(2,1)}) %all-gather.6.cloned.1.call-update) | async-done | bytes 2097168 | tf_op jit(solution)/shard_map/all_gather | solution.py:167
  379.5 5.2 %convolution_convert_fusion.3 = bf16[512,1024]{1,0:T(8,128)(2,1)S(1)} fusion(bf16[512,2048]{1,0:T(8,128)(2,1)} %all-gather.6.cloned.1.call-done, bf16[2048,1024]{1,0:T(8,128)(2,1)} %bitcast.143), kind=kOutput, calls=%fused_computation.49 | convolution fusion | flops 2148007936 | bytes 7340032 | tf_op jit(solution)/shard_map/dot_general | solution.py:166
  (131 shorter events, 66.3 us)
Async XLA Ops:
  7.2 40.8 %all-gather.8.cloned.1.call-start = ((), (), s32[]{:S(2)}) async-start(), calls=%async_computation.10 | async-start | bytes 1474560 | tf_op jit(solution)/shard_map/all_gather | solution.py:71
  17.8 41.4 %all-to-all-start = ((bf16[8,64,2048]{2,1,0:T(8,128)(2,1)}), bf16[8,64,2048]{2,1,0:T(8,128)(2,1)}, u32[]{:S(2)}, u32[]{:S(2)}) async-start(bf16[8,64,2048]{2,1,0:T(8,128)(2,1)} %bitcast.2), calls=%async_computation | async-start | bytes 4194304 | tf_op jit(solution)/shard_map/all_to_all | solution.py:107
  59.2 48.8 %all-to-all-start.1 = ((bf16[8,192,1024]{2,1,0:T(8,128)(2,1)}), bf16[8,192,1024]{2,1,0:T(8,128)(2,1)}, u32[]{:S(2)}, u32[]{:S(2)}) async-start(bf16[8,192,1024]{2,1,0:T(8,128)(2,1)} %bitcast.12), calls=%async_computation.1 | async-start | bytes 6291456 | tf_op jit(solution)/shard_map/all_to_all | solution.py:107
  63.7 39.3 %all-gather.10.cloned.1.call-start = ((), (), s32[]{:S(2)}) async-start(), calls=%async_computation.11 | async-start | bytes 1310720 | tf_op jit(solution)/shard_map/all_gather | solution.py:72
  75.8 8.8 %copy-start.5 = (f32[1,16,12]{1,0,2:T(1,128)S(1)}, f32[1,16,12]{1,0,2:T(1,128)}, u32[]{:S(2)}) copy-start(f32[1,16,12]{1,0,2:T(1,128)} %param.19) | copy-start | bytes 2308
  75.8 9.1 %copy-start.6 = (f32[1,6,16]{2,0,1:T(1,128)S(1)}, f32[1,6,16]{2,0,1:T(1,128)}, u32[]{:S(2)}) copy-start(f32[1,6,16]{2,0,1:T(1,128)} %param.21) | copy-start | bytes 1156
  84.9 7.9 %slice-start = ((s8[6291456]{0:T(1024)(128)(4,1)}), s8[4194304]{0:T(1024)(128)(4,1)S(1)}, s32[]{:S(2)}) async-start(s8[6291456]{0:T(1024)(128)(4,1)} %bitcast.124), calls=%async_computation.12 | async-start | bytes 8388608
  84.9 7.9 %slice-start.1 = ((s8[6291456]{0:T(1024)(128)(4,1)}), s8[2097152]{0:T(1024)(128)(4,1)S(1)}, s32[]{:S(2)}) async-start(s8[6291456]{0:T(1024)(128)(4,1)} %bitcast.124), calls=%async_computation.13 | async-start | bytes 4194304
  108.1 41.7 %all-to-all-start.2 = ((bf16[8,192,1024]{2,1,0:T(8,128)(2,1)}), bf16[8,192,1024]{2,1,0:T(8,128)(2,1)S(1)}, u32[]{:S(2)}, u32[]{:S(2)}) async-start(bf16[8,192,1024]{2,1,0:T(8,128)(2,1)} %bitcast.20), calls=%async_computation.2 | async-start | bytes 6291456 | tf_op jit(solution)/shard_map/all_to_all | solution.py:107
  111.9 5.9 %slice-start.4 = ((s8[6291456]{0:T(1024)(128)(4,1)}), s8[4194304]{0:T(1024)(128)(4,1)S(1)}, s32[]{:S(2)}) async-start(s8[6291456]{0:T(1024)(128)(4,1)} %bitcast.138), calls=%async_computation.16 | async-start | bytes 8388608
  113.7 4.1 %slice-start.5 = ((s8[6291456]{0:T(1024)(128)(4,1)}), s8[2097152]{0:T(1024)(128)(4,1)S(1)}, s32[]{:S(2)}) async-start(s8[6291456]{0:T(1024)(128)(4,1)} %bitcast.138), calls=%async_computation.17 | async-start | bytes 4194304
  113.7 10.7 %slice-start.2 = ((s8[6291456]{0:T(1024)(128)(4,1)}), s8[2097152]{0:T(1024)(128)(4,1)S(1)}, s32[]{:S(2)}) async-start(s8[6291456]{0:T(1024)(128)(4,1)} %bitcast.136), calls=%async_computation.14 | async-start | bytes 4194304
  117.8 6.6 %slice-start.3 = ((s8[6291456]{0:T(1024)(128)(4,1)}), s8[4194304]{0:T(1024)(128)(4,1)S(1)}, s32[]{:S(2)}) async-start(s8[6291456]{0:T(1024)(128)(4,1)} %bitcast.136), calls=%async_computation.15 | async-start | bytes 8388608
  158.4 2.0 copy-start.4
  167.1 5.9 %copy-start.1 = (bf16[2048,768]{1,0:T(8,128)(2,1)}, bf16[2048,768]{1,0:T(8,128)(2,1)S(1)}, u32[]{:S(2)}) copy-start(bf16[2048,768]{1,0:T(8,128)(2,1)S(1)} %bitcast_select_fusion) | copy-start | bytes 9437188
  173.0 59.4 %all-to-all-start.3 = ((bf16[8,256,1152]{2,1,0:T(8,128)(2,1)}), bf16[8,256,1152]{2,1,0:T(8,128)(2,1)}, u32[]{:S(2)}, u32[]{:S(2)}) async-start(bf16[8,256,1152]{2,1,0:T(8,128)(2,1)} %bitcast.141), calls=%async_computation.3 | async-start | bytes 9437184 | tf_op jit(solution)/shard_map/all_to_all | solution.py:107
  177.7 117.6 %reduce-scatter.3.cloned.1.call-start = ((), (), s32[]{:S(2)}) async-start(), calls=%async_computation.7 | async-start | bytes 2949120 | tf_op jit(solution)/shard_map/reduce_scatter | solution.py:161
  240.3 92.0 %reduce-scatter.5.cloned.1.call-start = ((), (), s32[]{:S(2)}) async-start(), calls=%async_computation.8 | async-start | bytes 2293760 | tf_op jit(solution)/shard_map/reduce_scatter | solution.py:161
  293.0 2.1 copy-start
  295.0 84.4 %all-gather.6.cloned.1.call-start = ((), (), s32[]{:S(2)}) async-start(), calls=%async_computation.9 | async-start | bytes 2621440 | tf_op jit(solution)/shard_map/all_gather | solution.py:167
  334.2 5.4 %copy-start.8 = (s32[21]{0:T(128)S(1)}, s32[21]{0:T(128)}, u32[]{:S(2)}) copy-start(s32[21]{0:T(128)} %param.25) | copy-start | bytes 256
  334.2 5.4 %copy-start.7 = (s32[1,2,256]{2,1,0:T(2,128)S(1)}, s32[1,2,256]{2,1,0:T(2,128)}, u32[]{:S(2)}) copy-start(s32[1,2,256]{2,1,0:T(2,128)} %param.24) | copy-start | bytes 6148
  389.4 3.6 collective-permute-start
  393.0 4.4 %collective-permute-start.1 = (f32[21]{0:T(128)S(1)}, f32[21]{0:T(128)S(1)}, u32[]{:S(2)}, u32[]{:S(2)}) collective-permute-start(f32[21]{0:T(128)S(1)} %add.131), channel_id=1, source_target_pairs={{0,2},{1,3},{2,0},{3,1},{4,6},{5,7},{6,4},{7,5},{8,10},{9,11},{10,... | collective-permute-start | bytes 260 | tf_op jit(solution)/shard_map/ppermute | solution.py:211
  (3 other events, 4.8 us)
Sparse Core Ops, SparseCore 0:
  14.7 33.1 all-gather.7
  75.9 27.0 all-gather.9
  240.4 45.7 reduce-scatter.2
  295.2 37.0 reduce-scatter.4
  334.4 45.0 all-gather.5

commit v2 on v1

--- a/solution.py
+++ b/solution.py
@@ -204,12 +204,15 @@
     counts = (frames - jnp.abs(lag_offsets)).astype(jnp.float32)
     score = sums / jnp.sqrt(counts * head_size)[None, :]
     partial_logits = jnp.sum(head_weight[:, None] * score, axis=0)
-    sync_logits = partial_logits
-    step = 1
-    while step < lines:
-        pairs = [(i, i ^ step) for i in range(lines)]
-        sync_logits = sync_logits + lax.ppermute(sync_logits, "tensor", pairs)
-        step *= 2
+    received = [partial_logits] + [
+        lax.ppermute(partial_logits, "tensor", [(i, (i + k) % lines) for i in range(lines)])
+        for k in range(1, lines)
+    ]
+    stacked = jnp.stack(received)
+    ordered = jnp.take(stacked, (here - jnp.arange(lines, dtype=jnp.int32)) % lines, axis=0)
+    sync_logits = ordered[0]
+    for j in range(1, lines):
+        sync_logits = sync_logits + ordered[j]
     return (mixed, sync_logits[None, :])
 
 

time: 409 us -> 408 us (level)
    ppermute x2 -> x3, waiting for transfers between devices: 6.93 us -> 1.94 us  [shards(): lax.ppermute(partial_logits, 'tensor', [(i, (i + k) % lines) for i in ran...]
  transfers between devices with their start and end apart: 11 -> 12, of which waited for: 8 -> 8; matrix products, arithmetic and copies ran while one was open for 21% -> 21% of each run, Pallas kernels for 0% -> 0%
where the time goes in v2:
time: 408 us; the launch traced here: 403 us
  waiting for transfers between devices  173 us (42%)
  matrix products  60.1 us (15%)
  blocking collectives  45.9 us (11%)
  other arithmetic  40.8 us (10%)
  local copies, waits for them, and re-layouts  34.9 us (9%)
  starting transfers between devices  34.3 us (8%)
  between operations  14.5 us (4%)
    all_to_all x4, waiting for transfers between devices, send(): lax.all_to_all(part.reshape(plane, depth, part.shape[-1]), group, split_a...  64.1 us
    all_to_all x1, blocking collectives, send(): lax.all_to_all(part.reshape(plane, depth, part.shape[-1]), group, split_a...  45.9 us
    all_gather x1, waiting for transfers between devices, shards(): lax.all_gather(mixed, 'tensor', axis=0, tiled=True)  39.8 us
    reduce_scatter x2, waiting for transfers between devices, shards(): lax.psum_scatter(mixed_parts[h], 'tensor', scatter_dimension=0, tiled=True)  36 us
    all_gather x1, waiting for transfers between devices, shards(): line_a = lax.all_gather(packed, 'tensor', axis=0, tiled=False)  24.9 us
    all_to_all x4, starting transfers between devices, send(): lax.all_to_all(part.reshape(plane, depth, part.shape[-1]), group, split_a...  17.9 us
    unnamed x42, local copies, waits for them, and re-layouts  16.5 us
    convert_element_type x3, other arithmetic, dequant(): return (weights.astype(jnp.float32) * full).astype(jnp.bfloat16)  16.4 us
  transfers between devices with their start and end apart: 12, of which 8 were waited for; matrix products, arithmetic and copies ran while one was open for 21% of the time, Pallas kernels for 0%

profile of v2, /device:TPU:0, one launch (start us, length us, event | category | flops | bytes accessed | tf_op | source)
XLA Modules:
  0.0 403.2 jit_solution(12658422469973661733)
XLA Ops:
  17.8 5.2 %all-to-all-start = ((bf16[8,64,2048]{2,1,0:T(8,128)(2,1)}), bf16[8,64,2048]{2,1,0:T(8,128)(2,1)}, u32[]{:S(2)}, u32[]{:S(2)}) async-start(bf16[8,64,2048]{2,1,0:T(8,128)(2,1)} %bitcast.2), calls=%async_computation | async-start | bytes 4194304 | tf_op jit(solution)/shard_map/all_to_all | solution.py:107
  23.0 24.9 %all-gather.8.cloned.1.call-done = bf16[576,1024]{1,0:T(8,128)(2,1)} async-done(((bf16[144,1024]{1,0:T(8,128)(2,1)}), bf16[576,1024]{1,0:T(8,128)(2,1)}) %all-gather.8.cloned.1.call-update) | async-done | bytes 1179664 | tf_op jit(solution)/shard_map/all_gather | solution.py:71
  59.2 4.5 %all-to-all-start.1 = ((bf16[8,192,1024]{2,1,0:T(8,128)(2,1)}), bf16[8,192,1024]{2,1,0:T(8,128)(2,1)}, u32[]{:S(2)}, u32[]{:S(2)}) async-start(bf16[8,192,1024]{2,1,0:T(8,128)(2,1)} %bitcast.12), calls=%async_computation.1 | async-start | bytes 6291456 | tf_op jit(solution)/shard_map/all_to_all | solution.py:107
  63.7 12.1 %all-gather.10.cloned.1.call-start = ((), (), s32[]{:S(2)}) async-start(), calls=%async_computation.11 | async-start | bytes 1310720 | tf_op jit(solution)/shard_map/all_gather | solution.py:72
  75.8 8.7 %copy.107 = bf16[1,2048,1536]{1,2,0:T(8,128)(2,1)} copy(bf16[1,2048,1536]{2,1,0:T(8,128)(2,1)} %param.18) | data formatting | bytes 12582912 | tf_op args[4]
  84.9 7.8 %fusion = bf16[2048,1536]{0,1:T(8,128)(2,1)} fusion(f32[2048,12]{0,1:T(8,128)S(1)} %bitcast.153, bf16[1,2048,1536]{1,2,0:T(8,128)(2,1)} %copy.107), kind=kLoop, calls=%fused_computation.6 | loop fusion | flops 9437184 | bytes 12681216 | tf_op jit(solution)/shard_map/convert_element_type | solution.py:10
  92.8 4.5 %multiply_convert_fusion = bf16[2048,12,128]{0,2,1:T(8,128)(2,1)} fusion(f32[2048,12]{0,1:T(8,128)S(1)} %bitcast.154, bf16[2048,12,128]{0,2,1:T(8,128)(2,1)S(1)} %bitcast.130), kind=kLoop, calls=%fused_computation.7 | loop fusion | flops 9437184 | bytes 12681216 | tf_op jit(solution)/shard_map/convert_element_type | solution.py:10
  97.3 5.8 %all-gather.10.cloned.1.call-done = bf16[512,1024]{1,0:T(8,128)(2,1)} async-done(((bf16[128,1024]{1,0:T(8,128)(2,1)}), bf16[512,1024]{1,0:T(8,128)(2,1)}) %all-gather.10.cloned.1.call-update) | async-done | bytes 1048592 | tf_op jit(solution)/shard_map/all_gather | solution.py:72
  113.7 4.1 %fusion.2 = bf16[768,2048]{1,0:T(8,128)(2,1)} fusion(f32[96,8,16,128]{3,2,1,0:T(8,128)S(1)} %bitcast.131, bf16[1,768,2048]{2,1,0:T(8,128)(2,1)S(1)} %copy-done.2), kind=kLoop, calls=%fused_computation.15 | loop fusion | flops 4718592 | bytes 12582912 | tf_op jit(solution)/shard_map/convert_element_type | solution.py:10
  117.8 5.2 %fusion.102 = f32[512,1536]{1,0:T(8,128)S(1)} fusion(bf16[512,2048]{1,0:T(8,128)(2,1)} %bitcast.3, bf16[2048,1536]{0,1:T(8,128)(2,1)S(1)} %bitcast.144), kind=kOutput, calls=%fused_computation.175 | convolution fusion | flops 3221225472 | bytes 11534336 | tf_op jit(solution)/shard_map/dot_general | solution.py:129
  124.5 9.5 %fusion.25 = f32[1536,1536]{1,0:T(8,128)} fusion(bf16[1536,1024]{1,0:T(8,128)(2,1)} %bitcast.13, bf16[2048,1536]{0,1:T(8,128)(2,1)S(1)} %bitcast.141), kind=kOutput, calls=%fused_computation.35 | convolution fusion | flops 4831838208 | bytes 15728640 | tf_op jit(solution)/shard_map/dot_general | solution.py:131
  133.9 15.8 %all-to-all-done.2 = bf16[8,192,1024]{2,1,0:T(8,128)(2,1)S(1)} async-done(((bf16[8,192,1024]{2,1,0:T(8,128)(2,1)}), bf16[8,192,1024]{2,1,0:T(8,128)(2,1)S(1)}, u32[]{:S(2)}, u32[]{:S(2)}) %all-to-all-start.2) | async-done | bytes 3145760 | tf_op jit(solution)/shard_map/all_to_all | solution.py:107
  149.7 8.6 %convolution_add_fusion = f32[1536,1536]{1,0:T(8,128)S(1)} fusion(f32[1536,1536]{1,0:T(8,128)} %fusion.25, bf16[1536,1024]{1,0:T(8,128)(2,1)S(1)} %bitcast.149, bf16[2048,1536]{0,1:T(8,128)(2,1)} %fusion), kind=kOutput, calls=%fused_computation.8 | convolution fusion | flops 4834197504 | bytes 25165824 | tf_op jit(solution)/shard_map/dot_general | solution.py:132
  167.1 5.9 %convolution_convert_fusion = bf16[2048,1152]{1,0:T(8,128)(2,1)} fusion(bf16[2048,768]{1,0:T(8,128)(2,1)S(1)} %bitcast_select_fusion, bf16[768,2048]{1,0:T(8,128)(2,1)S(1)} %copy-done.3), kind=kOutput, calls=%fused_computation.13 | convolution fusion | flops 3626237952 | bytes 9633792 | tf_op jit(solution)/shard_map/dot_general | solution.py:148
  173.0 4.6 %all-to-all-start.3 = ((bf16[8,256,1152]{2,1,0:T(8,128)(2,1)}), bf16[8,256,1152]{2,1,0:T(8,128)(2,1)}, u32[]{:S(2)}, u32[]{:S(2)}) async-start(bf16[8,256,1152]{2,1,0:T(8,128)(2,1)} %bitcast.145), calls=%async_computation.3 | async-start | bytes 9437184 | tf_op jit(solution)/shard_map/all_to_all | solution.py:107
  178.0 6.0 %select_reduce_fusion.1 = (bf16[4,512,128]{2,1,0:T(8,128)(2,1)S(1)}, bf16[4,512,128]{2,1,0:T(8,128)(2,1)S(1)}) fusion(f32[4,128,8]{1,2,0:T(8,128)S(1)} %convert_element_type.163, s32[4,128,8]{1,2,0:T(8,128)S(1)} %copy.100, f32[4,128,8]{1,2,0:T(8,128)S(1)} %convert_element_type.188), kind=kLoop, calls=%fused_computation.10 | loop fusion | flops 9961472 | bytes 1097728 | tf_op jit(solution)/shard_map/reduce_sum | solution.py:85
  184.0 48.3 %all-to-all-done.3 = bf16[8,256,1152]{2,1,0:T(8,128)(2,1)} async-done(((bf16[8,256,1152]{2,1,0:T(8,128)(2,1)}), bf16[8,256,1152]{2,1,0:T(8,128)(2,1)}, u32[]{:S(2)}, u32[]{:S(2)}) %all-to-all-start.3) | async-done | bytes 4718624 | tf_op jit(solution)/shard_map/all_to_all | solution.py:107
  235.6 4.6 %fusion.14 = f32[4,128,1152]{2,1,0:T(8,128)} fusion(f32[4,128,1152]{2,1,0:T(8,128)S(1)} %fusion.17, bf16[4,8,64,128]{3,2,1,0:T(8,128)(2,1)S(1)} %bitcast.136, bf16[8,4,64,1152]{3,2,1,0:T(8,128)(2,1)} %bitcast.29), kind=kOutput, calls=%fused_computation.28 | convolution fusion | flops 604569600 | bytes 9961472 | tf_op jit(solution)/shard_map/bpsr,pbsd->brd/dot_general | solution.py:155
  240.5 5.7 %convolution_convert_fusion.1 = bf16[2048,896]{1,0:T(8,128)(2,1)S(1)} fusion(bf16[2048,768]{1,0:T(8,128)(2,1)} %copy-done.1, bf16[768,2048]{1,0:T(8,128)(2,1)} %fusion.2), kind=kOutput, calls=%fused_computation.26 | convolution fusion | flops 2820407296 | bytes 8192000 | tf_op jit(solution)/shard_map/dot_general | solution.py:148
  246.2 45.9 %all_to_all.25 = bf16[8,256,896]{2,1,0:T(8,128)(2,1)S(1)} all-to-all(bf16[8,256,896]{2,1,0:T(8,128)(2,1)S(1)} %bitcast.148), channel_id=1, replica_groups=mesh['dp'=4,'expert'=2,'tensor'=4] {'dp','expert'}, dimensions={0} | all-to-all | bytes 7340032 | tf_op jit(solution)/shard_map/all_to_all | solution.py:107
  296.3 36.0 %reduce-scatter.5.cloned.1.call-done = f32[128,896]{1,0:T(8,128)} async-done(((f32[512,896]{1,0:T(8,128)}), f32[128,896]{1,0:T(8,128)}) %reduce-scatter.5.cloned.1.call-update) | async-done | bytes 458768 | tf_op jit(solution)/shard_map/reduce_scatter | solution.py:161
  334.2 5.3 %copy.134 = bf16[256,8,2,512]{3,1,2,0:T(8,128)(2,1)} copy(bf16[256,8,2,512]{3,2,1,0:T(2,128)(2,1)} %bitcast.146) | data formatting | bytes 8388608
  339.7 39.8 %all-gather.6.cloned.1.call-done = bf16[512,2048]{1,0:T(8,128)(2,1)} async-done(((bf16[128,2048]{1,0:T(8,128)(2,1)}), bf16[512,2048]{1,0:T(8,128)(2,1)}) %all-gather.6.cloned.1.call-update) | async-done | bytes 2097168 | tf_op jit(solution)/shard_map/all_gather | solution.py:167
  379.5 5.2 %convolution_convert_fusion.3 = bf16[512,1024]{1,0:T(8,128)(2,1)S(1)} fusion(bf16[512,2048]{1,0:T(8,128)(2,1)} %all-gather.6.cloned.1.call-done, bf16[2048,1024]{1,0:T(8,128)(2,1)} %bitcast.147), kind=kOutput, calls=%fused_computation.50 | convolution fusion | flops 2148007936 | bytes 7340032 | tf_op jit(solution)/shard_map/dot_general | solution.py:166
  (137 shorter events, 64.7 us)
Async XLA Ops:
  7.2 40.8 %all-gather.8.cloned.1.call-start = ((), (), s32[]{:S(2)}) async-start(), calls=%async_computation.10 | async-start | bytes 1474560 | tf_op jit(solution)/shard_map/all_gather | solution.py:71
  17.8 41.4 %all-to-all-start = ((bf16[8,64,2048]{2,1,0:T(8,128)(2,1)}), bf16[8,64,2048]{2,1,0:T(8,128)(2,1)}, u32[]{:S(2)}, u32[]{:S(2)}) async-start(bf16[8,64,2048]{2,1,0:T(8,128)(2,1)} %bitcast.2), calls=%async_computation | async-start | bytes 4194304 | tf_op jit(solution)/shard_map/all_to_all | solution.py:107
  59.2 49.0 %all-to-all-start.1 = ((bf16[8,192,1024]{2,1,0:T(8,128)(2,1)}), bf16[8,192,1024]{2,1,0:T(8,128)(2,1)}, u32[]{:S(2)}, u32[]{:S(2)}) async-start(bf16[8,192,1024]{2,1,0:T(8,128)(2,1)} %bitcast.12), calls=%async_computation.1 | async-start | bytes 6291456 | tf_op jit(solution)/shard_map/all_to_all | solution.py:107
  63.7 39.5 %all-gather.10.cloned.1.call-start = ((), (), s32[]{:S(2)}) async-start(), calls=%async_computation.11 | async-start | bytes 1310720 | tf_op jit(solution)/shard_map/all_gather | solution.py:72
  75.8 8.8 %copy-start.5 = (f32[1,16,12]{1,0,2:T(1,128)S(1)}, f32[1,16,12]{1,0,2:T(1,128)}, u32[]{:S(2)}) copy-start(f32[1,16,12]{1,0,2:T(1,128)} %param.19) | copy-start | bytes 2308
  75.8 9.1 %copy-start.6 = (f32[1,6,16]{2,0,1:T(1,128)S(1)}, f32[1,6,16]{2,0,1:T(1,128)}, u32[]{:S(2)}) copy-start(f32[1,6,16]{2,0,1:T(1,128)} %param.21) | copy-start | bytes 1156
  84.9 7.9 %slice-start = ((s8[6291456]{0:T(1024)(128)(4,1)}), s8[4194304]{0:T(1024)(128)(4,1)S(1)}, s32[]{:S(2)}) async-start(s8[6291456]{0:T(1024)(128)(4,1)} %bitcast.128), calls=%async_computation.12 | async-start | bytes 8388608
  84.9 7.9 %slice-start.1 = ((s8[6291456]{0:T(1024)(128)(4,1)}), s8[2097152]{0:T(1024)(128)(4,1)S(1)}, s32[]{:S(2)}) async-start(s8[6291456]{0:T(1024)(128)(4,1)} %bitcast.128), calls=%async_computation.13 | async-start | bytes 4194304
  108.2 41.5 %all-to-all-start.2 = ((bf16[8,192,1024]{2,1,0:T(8,128)(2,1)}), bf16[8,192,1024]{2,1,0:T(8,128)(2,1)S(1)}, u32[]{:S(2)}, u32[]{:S(2)}) async-start(bf16[8,192,1024]{2,1,0:T(8,128)(2,1)} %bitcast.20), calls=%async_computation.2 | async-start | bytes 6291456 | tf_op jit(solution)/shard_map/all_to_all | solution.py:107
  111.9 5.9 %slice-start.4 = ((s8[6291456]{0:T(1024)(128)(4,1)}), s8[4194304]{0:T(1024)(128)(4,1)S(1)}, s32[]{:S(2)}) async-start(s8[6291456]{0:T(1024)(128)(4,1)} %bitcast.142), calls=%async_computation.16 | async-start | bytes 8388608
  113.7 4.1 %slice-start.5 = ((s8[6291456]{0:T(1024)(128)(4,1)}), s8[2097152]{0:T(1024)(128)(4,1)S(1)}, s32[]{:S(2)}) async-start(s8[6291456]{0:T(1024)(128)(4,1)} %bitcast.142), calls=%async_computation.17 | async-start | bytes 4194304
  113.7 10.7 %slice-start.2 = ((s8[6291456]{0:T(1024)(128)(4,1)}), s8[2097152]{0:T(1024)(128)(4,1)S(1)}, s32[]{:S(2)}) async-start(s8[6291456]{0:T(1024)(128)(4,1)} %bitcast.140), calls=%async_computation.14 | async-start | bytes 4194304
  117.8 6.6 %slice-start.3 = ((s8[6291456]{0:T(1024)(128)(4,1)}), s8[4194304]{0:T(1024)(128)(4,1)S(1)}, s32[]{:S(2)}) async-start(s8[6291456]{0:T(1024)(128)(4,1)} %bitcast.140), calls=%async_computation.15 | async-start | bytes 8388608
  167.1 5.9 %copy-start.1 = (bf16[2048,768]{1,0:T(8,128)(2,1)}, bf16[2048,768]{1,0:T(8,128)(2,1)S(1)}, u32[]{:S(2)}) copy-start(bf16[2048,768]{1,0:T(8,128)(2,1)S(1)} %bitcast_select_fusion) | copy-start | bytes 9437188
  173.0 59.4 %all-to-all-start.3 = ((bf16[8,256,1152]{2,1,0:T(8,128)(2,1)}), bf16[8,256,1152]{2,1,0:T(8,128)(2,1)}, u32[]{:S(2)}, u32[]{:S(2)}) async-start(bf16[8,256,1152]{2,1,0:T(8,128)(2,1)} %bitcast.145), calls=%async_computation.3 | async-start | bytes 9437184 | tf_op jit(solution)/shard_map/all_to_all | solution.py:107
  177.6 117.5 %reduce-scatter.3.cloned.1.call-start = ((), (), s32[]{:S(2)}) async-start(), calls=%async_computation.7 | async-start | bytes 2949120 | tf_op jit(solution)/shard_map/reduce_scatter | solution.py:161
  240.3 92.0 %reduce-scatter.5.cloned.1.call-start = ((), (), s32[]{:S(2)}) async-start(), calls=%async_computation.8 | async-start | bytes 2293760 | tf_op jit(solution)/shard_map/reduce_scatter | solution.py:161
  292.9 2.1 copy-start
  295.0 84.5 %all-gather.6.cloned.1.call-start = ((), (), s32[]{:S(2)}) async-start(), calls=%async_computation.9 | async-start | bytes 2621440 | tf_op jit(solution)/shard_map/all_gather | solution.py:167
  334.2 5.4 %copy-start.8 = (s32[21]{0:T(128)S(1)}, s32[21]{0:T(128)}, u32[]{:S(2)}) copy-start(s32[21]{0:T(128)} %param.25) | copy-start | bytes 256
  334.2 5.4 %copy-start.7 = (s32[1,2,256]{2,1,0:T(2,128)S(1)}, s32[1,2,256]{2,1,0:T(2,128)}, u32[]{:S(2)}) copy-start(s32[1,2,256]{2,1,0:T(2,128)} %param.24) | copy-start | bytes 6148
  389.4 5.4 %collective-permute-start = (f32[21]{0:T(128)S(1)}, f32[21]{0:T(128)S(1)}, u32[]{:S(2)}, u32[]{:S(2)}) collective-permute-start(f32[21]{0:T(128)S(1)} %fusion.48), channel_id=1, source_target_pairs={{0,1},{1,2},{2,3},{3,0},{4,5},{5,6},{6,7},{7,4},{8,9},{9,10},{10,1... | collective-permute-start | bytes 260 | tf_op jit(solution)/shard_map/ppermute | solution.py:208
  389.5 5.3 %collective-permute-start.1 = (f32[21]{0:T(128)S(1)}, f32[21]{0:T(128)S(1)}, u32[]{:S(2)}, u32[]{:S(2)}) collective-permute-start(f32[21]{0:T(128)S(1)} %fusion.48), channel_id=1, source_target_pairs={{0,2},{1,3},{2,0},{3,1},{4,6},{5,7},{6,4},{7,5},{8,10},{9,11},{10,... | collective-permute-start | bytes 260 | tf_op jit(solution)/shard_map/ppermute | solution.py:208
  391.2 4.2 %collective-permute-start.2 = (f32[21]{0:T(128)S(1)}, f32[21]{0:T(128)S(1)}, u32[]{:S(2)}, u32[]{:S(2)}) collective-permute-start(f32[21]{0:T(128)S(1)} %fusion.48), channel_id=1, source_target_pairs={{0,3},{1,0},{2,1},{3,2},{4,7},{5,4},{6,5},{7,6},{8,11},{9,8},{10,9... | collective-permute-start | bytes 260 | tf_op jit(solution)/shard_map/ppermute | solution.py:208
  (4 other events, 6.8 us)
Sparse Core Ops, SparseCore 0:
  14.7 33.1 all-gather.7
  75.9 27.1 all-gather.9
  240.4 45.7 reduce-scatter.2
  295.1 37.1 reduce-scatter.4
  334.3 45.0 all-gather.5
